TPU v7x, 256 devices: a whole 4x4x8 slice. The times are simulated.
256 devices in a mesh: sample: 8 (over z_lo, y), space: 32 (over x, z_hi, core).
Axes of the slice: x: 4, y: 4, z: 8 (z_hi: 4, z_lo: 2; z = z_hi * 2 + z_lo), core: 2. Of those that a mesh axis runs over, the one named last changes fastest.
Arguments:
- volume: bfloat16 [64, 8, 32, 1024], P('space', 'sample'), may hold values from -6 to 6
- out_grads: bfloat16 [32, 8, 128, 256], P('space', 'sample'), may hold values from -6 to 6
- kernel_one: bfloat16 [27, 32, 64], replicated, may hold values from -0.21875 to 0.21875
- kernel_two: bfloat16 [27, 64, 128], replicated, may hold values from -0.15625 to 0.15625
Outputs:
- layer_out: bfloat16 [32, 8, 128, 256], P('space', 'sample')
- input_grads: bfloat16 [64, 8, 32, 1024], P('space', 'sample')
- kernel_one_grads: float32 [27, 32, 64], replicated
- kernel_two_grads: float32 [27, 64, 128], replicated
All inputs are finite; a program needn't handle non-finite values.
Results may differ from a plain program's by a relative error of at most 0.015.
Values may be sent and summed in bfloat16 or wider, within the bound.
No kernel may reach another device: no remote copies, remote signals or barrier semaphores. Data moves between devices by JAX's collectives and lax.ppermute only.
A program may use at most 128 MiB of HBM per device.

v0:
```python
import jax
import jax.numpy as jnp
from jax import lax
from jax.sharding import PartitionSpec as P

SIDE = 32


def with_halo(block, sides, width):
    for axis, dim in sides:
        count = lax.axis_size(axis)
        forward = [(i, i + 1) for i in range(count - 1)]
        backward = [(target, source) for source, target in forward]
        low = lax.ppermute(
            lax.slice_in_dim(block, block.shape[dim] - width, None, axis=dim), axis, forward
        )
        high = lax.ppermute(lax.slice_in_dim(block, 0, width, axis=dim), axis, backward)
        block = jnp.concatenate([low, block, high], axis=dim)
    return block


def passed_along(block, axis, distance):
    devices = range(lax.axis_size(axis))
    route = [(i - distance, i) for i in devices if i - distance in devices]
    return lax.ppermute(block, axis, route)


def convolve(inputs, kernel, stride, margins, dilation):
    return lax.conv_general_dilated(
        inputs,
        kernel,
        (stride, stride, stride),
        margins,
        lhs_dilation=(dilation, dilation, dilation),
        dimension_numbers=("DNCHW", "DHWIO", "DNCHW"),
        preferred_element_type=jnp.float32,
    )


def kernel_cube(kernel):
    return kernel.reshape(3, 3, 3, kernel.shape[1], kernel.shape[2])


def reversed_kernel(kernel):
    cube = kernel_cube(kernel)
    return jnp.transpose(cube[::-1, ::-1, ::-1], (0, 1, 2, 4, 3))


def weight_grad(padded, grads, stride):
    depth_out, rows_out, cols_out = (grads.shape[0], grads.shape[3], grads.shape[4])
    terms = []
    for depth_tap in range(3):
        for row_tap in range(3):
            for col_tap in range(3):
                window = lax.slice(
                    padded,
                    (depth_tap, 0, 0, row_tap, col_tap),
                    (
                        depth_tap + stride * (depth_out - 1) + 1,
                        padded.shape[1],
                        padded.shape[2],
                        row_tap + stride * (rows_out - 1) + 1,
                        col_tap + stride * (cols_out - 1) + 1,
                    ),
                    (stride, 1, 1, stride, stride),
                )
                terms.append(
                    jnp.einsum("zbiyx,zboyx->io", window, grads, preferred_element_type=jnp.float32)
                )
    return jnp.stack(terms)


def local(volume, out_grads, kernel_one, kernel_two):
    depth, batch, channels_in, plane = volume.shape
    channels_two = kernel_two.shape[2]
    half_side = SIDE // 2
    space_count = lax.axis_size("space")
    sample_count = lax.axis_size("sample")
    scale_one = float(sample_count * batch * space_count * depth * plane) ** (-0.5)
    scale_two = scale_one * 8.0**0.5
    cells = volume.reshape(depth, batch, channels_in, SIDE, SIDE)
    grads_cells = out_grads.reshape(depth // 2, batch, channels_two, half_side, half_side)
    framed = with_halo(cells, (("space", 0),), 1)
    pre_one = convolve(framed, kernel_cube(kernel_one), 1, [(0, 0), (1, 1), (1, 1)], 1)
    hidden = jax.nn.silu(pre_one).astype(jnp.bfloat16)
    below = passed_along(hidden[-1:], "space", 1)
    stacked = jnp.pad(jnp.concatenate([below, hidden], 0), ((0, 0), (0, 0), (0, 0), (1, 1), (1, 1)))
    strided = convolve(stacked, kernel_cube(kernel_two), 2, [(0, 0), (0, 0), (0, 0)], 1)
    above = passed_along(grads_cells, "space", -1)
    spread = convolve(
        jnp.concatenate([grads_cells, above], 0),
        reversed_kernel(kernel_two),
        1,
        [(1, 0), (1, 2), (1, 2)],
        2,
    )
    hidden_grads = spread.astype(jnp.bfloat16)
    local_two = weight_grad(stacked, grads_cells, 2) * scale_two
    second_grads = lax.psum(local_two, ("sample", "space"))
    layer_out = strided.astype(jnp.bfloat16).reshape(depth // 2, batch, channels_two, plane // 4)
    sigma = jax.nn.sigmoid(pre_one)
    pre_grads = (hidden_grads.astype(jnp.float32) * sigma * (1.0 + pre_one * (1.0 - sigma))).astype(
        jnp.bfloat16
    )
    framed_grads = with_halo(pre_grads, (("space", 0),), 1)
    input_grads = convolve(
        framed_grads, reversed_kernel(kernel_one), 1, [(0, 0), (1, 1), (1, 1)], 1
    ).astype(jnp.bfloat16)
    padded_input = jnp.pad(framed, ((0, 0), (0, 0), (0, 0), (1, 1), (1, 1)))
    first_grads = weight_grad(padded_input, pre_grads, 1) * scale_one
    first_grads = lax.psum(first_grads, ("sample", "space"))
    return (
        layer_out,
        input_grads.reshape(depth, batch, channels_in, plane),
        first_grads,
        second_grads,
    )


def solution(mesh):
    in_specs = (P("space", "sample", None, None), P("space", "sample", None, None), P(), P())
    out_specs = (P("space", "sample", None, None), P("space", "sample", None, None), P(), P())
    return jax.shard_map(local, mesh=mesh, in_specs=in_specs, out_specs=out_specs, check_vma=False)
```

profile of v0, /device:TPU:1, one launch (start us, length us, event | category | flops | bytes accessed | tf_op | source)
XLA Modules:
  0.0 470.1 jit_solution(3152484372003187827)
XLA Ops:
  7.2 0.9 fusion.282
  8.8 5.1 %collective-permute-start.1 = (bf16[1,1,32,32,32]{3,2,0,4,1:T(8,128)(2,1)S(1)}, bf16[1,1,32,32,32]{3,2,0,4,1:T(8,128)(2,1)S(1)}, u32[]{:S(2)}, u32[]{:S(2)}) collective-permute-start(bf16[1,1,32,32,32]{3,2,0,4,1:T(8,128)(2,1)S(1)} %copy.119), channel_id=1, source_target_pairs={{1,0},{2,1},{3,2},{4,3},{5,4},{6,5},{7,6},{8,7},{9,8},{10,9},{11,1... | collective-permute-start | bytes 196616 | tf_op jit(solution)/shard_map/ppermute | solution.py:17
  14.6 3.1 collective-permute-start
  17.8 1.9 collective-permute-start.3
  20.5 0.9 copy.120
  21.4 1.6 copy.157
  24.1 1.6 copy.123
  25.7 1.2 slice.285
  27.0 3.8 add_divide_fusion
  31.0 4.5 collective-permute-start.2
  36.8 0.8 fusion.24
  38.5 1.9 collective-permute-start.5
  40.5 4.7 %collective-permute-start.4 = (bf16[1,1,64,32,32]{2,3,4,0,1:T(8,128)(2,1)S(1)}, bf16[1,1,64,32,32]{2,3,4,0,1:T(8,128)(2,1)}, u32[]{:S(2)}, u32[]{:S(2)}) collective-permute-start(bf16[1,1,64,32,32]{2,3,4,0,1:T(8,128)(2,1)S(1)} %get-tuple-element.21), channel_id=1, source_target_pairs={{0,1},{1,2},{2,3},{3,4},{4,5},{5,6},{6,7},{7,8},{8,9},{9,10},{10,1... | collective-permute-start | bytes 393224 | tf_op jit(solution)/shard_map/ppermute | solution.py:14
  59.3 0.8 broadcast_multiply_fusion.1
  60.6 5.1 %slice.246 = bf16[1,1,64,16,16]{2,3,4,1,0:T(8,128)(2,1)} slice(bf16[3,1,64,34,34]{2,3,4,1,0:T(8,128)(2,1)S(1)} %pad.9), slice={[0:1:1], [0:1:1], [0:64:1], [0:31:2], [0:31:2]} | slice | bytes 65536 | tf_op jit(solution)/shard_map/slice | solution.py:55
  65.7 4.9 %slice.247 = bf16[1,1,64,16,16]{2,3,4,1,0:T(8,128)(2,1)} slice(bf16[3,1,64,34,34]{2,3,4,1,0:T(8,128)(2,1)S(1)} %pad.9), slice={[0:1:1], [0:1:1], [0:64:1], [0:31:2], [1:32:2]} | slice | bytes 65536 | tf_op jit(solution)/shard_map/slice | solution.py:55
  70.6 4.9 %slice.248 = bf16[1,1,64,16,16]{2,3,4,1,0:T(8,128)(2,1)} slice(bf16[3,1,64,34,34]{2,3,4,1,0:T(8,128)(2,1)S(1)} %pad.9), slice={[0:1:1], [0:1:1], [0:64:1], [0:31:2], [2:33:2]} | slice | bytes 65536 | tf_op jit(solution)/shard_map/slice | solution.py:55
  75.5 4.9 %slice.249 = bf16[1,1,64,16,16]{2,3,4,1,0:T(8,128)(2,1)} slice(bf16[3,1,64,34,34]{2,3,4,1,0:T(8,128)(2,1)S(1)} %pad.9), slice={[0:1:1], [0:1:1], [0:64:1], [1:32:2], [0:31:2]} | slice | bytes 65536 | tf_op jit(solution)/shard_map/slice | solution.py:55
  80.4 4.9 %slice.250 = bf16[1,1,64,16,16]{2,3,4,1,0:T(8,128)(2,1)} slice(bf16[3,1,64,34,34]{2,3,4,1,0:T(8,128)(2,1)S(1)} %pad.9), slice={[0:1:1], [0:1:1], [0:64:1], [1:32:2], [1:32:2]} | slice | bytes 65536 | tf_op jit(solution)/shard_map/slice | solution.py:55
  85.2 4.9 %slice.251 = bf16[1,1,64,16,16]{2,3,4,1,0:T(8,128)(2,1)} slice(bf16[3,1,64,34,34]{2,3,4,1,0:T(8,128)(2,1)S(1)} %pad.9), slice={[0:1:1], [0:1:1], [0:64:1], [1:32:2], [2:33:2]} | slice | bytes 65536 | tf_op jit(solution)/shard_map/slice | solution.py:55
  90.1 4.9 %slice.252 = bf16[1,1,64,16,16]{2,3,4,1,0:T(8,128)(2,1)} slice(bf16[3,1,64,34,34]{2,3,4,1,0:T(8,128)(2,1)S(1)} %pad.9), slice={[0:1:1], [0:1:1], [0:64:1], [2:33:2], [0:31:2]} | slice | bytes 65536 | tf_op jit(solution)/shard_map/slice | solution.py:55
  95.0 4.9 %slice.253 = bf16[1,1,64,16,16]{2,3,4,1,0:T(8,128)(2,1)} slice(bf16[3,1,64,34,34]{2,3,4,1,0:T(8,128)(2,1)S(1)} %pad.9), slice={[0:1:1], [0:1:1], [0:64:1], [2:33:2], [1:32:2]} | slice | bytes 65536 | tf_op jit(solution)/shard_map/slice | solution.py:55
  99.9 4.9 %slice.254 = bf16[1,1,64,16,16]{2,3,4,1,0:T(8,128)(2,1)} slice(bf16[3,1,64,34,34]{2,3,4,1,0:T(8,128)(2,1)S(1)} %pad.9), slice={[0:1:1], [0:1:1], [0:64:1], [2:33:2], [2:33:2]} | slice | bytes 65536 | tf_op jit(solution)/shard_map/slice | solution.py:55
  104.8 4.9 %slice.255 = bf16[1,1,64,16,16]{2,3,4,1,0:T(8,128)(2,1)} slice(bf16[3,1,64,34,34]{2,3,4,1,0:T(8,128)(2,1)S(1)} %pad.9), slice={[1:2:1], [0:1:1], [0:64:1], [0:31:2], [0:31:2]} | slice | bytes 65536 | tf_op jit(solution)/shard_map/slice | solution.py:55
  109.6 4.9 %slice.256 = bf16[1,1,64,16,16]{2,3,4,1,0:T(8,128)(2,1)} slice(bf16[3,1,64,34,34]{2,3,4,1,0:T(8,128)(2,1)S(1)} %pad.9), slice={[1:2:1], [0:1:1], [0:64:1], [0:31:2], [1:32:2]} | slice | bytes 65536 | tf_op jit(solution)/shard_map/slice | solution.py:55
  114.5 4.9 %slice.257 = bf16[1,1,64,16,16]{2,3,4,1,0:T(8,128)(2,1)} slice(bf16[3,1,64,34,34]{2,3,4,1,0:T(8,128)(2,1)S(1)} %pad.9), slice={[1:2:1], [0:1:1], [0:64:1], [0:31:2], [2:33:2]} | slice | bytes 65536 | tf_op jit(solution)/shard_map/slice | solution.py:55
  119.4 4.9 %slice.258 = bf16[1,1,64,16,16]{2,3,4,1,0:T(8,128)(2,1)} slice(bf16[3,1,64,34,34]{2,3,4,1,0:T(8,128)(2,1)S(1)} %pad.9), slice={[1:2:1], [0:1:1], [0:64:1], [1:32:2], [0:31:2]} | slice | bytes 65536 | tf_op jit(solution)/shard_map/slice | solution.py:55
  124.3 4.9 %slice.259 = bf16[1,1,64,16,16]{2,3,4,1,0:T(8,128)(2,1)} slice(bf16[3,1,64,34,34]{2,3,4,1,0:T(8,128)(2,1)S(1)} %pad.9), slice={[1:2:1], [0:1:1], [0:64:1], [1:32:2], [1:32:2]} | slice | bytes 65536 | tf_op jit(solution)/shard_map/slice | solution.py:55
  129.2 4.9 %slice.260 = bf16[1,1,64,16,16]{2,3,4,1,0:T(8,128)(2,1)} slice(bf16[3,1,64,34,34]{2,3,4,1,0:T(8,128)(2,1)S(1)} %pad.9), slice={[1:2:1], [0:1:1], [0:64:1], [1:32:2], [2:33:2]} | slice | bytes 65536 | tf_op jit(solution)/shard_map/slice | solution.py:55
  134.0 4.9 %slice.261 = bf16[1,1,64,16,16]{2,3,4,1,0:T(8,128)(2,1)} slice(bf16[3,1,64,34,34]{2,3,4,1,0:T(8,128)(2,1)S(1)} %pad.9), slice={[1:2:1], [0:1:1], [0:64:1], [2:33:2], [0:31:2]} | slice | bytes 65536 | tf_op jit(solution)/shard_map/slice | solution.py:55
  138.9 4.9 %slice.262 = bf16[1,1,64,16,16]{2,3,4,1,0:T(8,128)(2,1)} slice(bf16[3,1,64,34,34]{2,3,4,1,0:T(8,128)(2,1)S(1)} %pad.9), slice={[1:2:1], [0:1:1], [0:64:1], [2:33:2], [1:32:2]} | slice | bytes 65536 | tf_op jit(solution)/shard_map/slice | solution.py:55
  143.8 4.9 %slice.263 = bf16[1,1,64,16,16]{2,3,4,1,0:T(8,128)(2,1)} slice(bf16[3,1,64,34,34]{2,3,4,1,0:T(8,128)(2,1)S(1)} %pad.9), slice={[1:2:1], [0:1:1], [0:64:1], [2:33:2], [2:33:2]} | slice | bytes 65536 | tf_op jit(solution)/shard_map/slice | solution.py:55
  148.7 4.9 %slice.264 = bf16[1,1,64,16,16]{2,3,4,1,0:T(8,128)(2,1)} slice(bf16[3,1,64,34,34]{2,3,4,1,0:T(8,128)(2,1)S(1)} %pad.9), slice={[2:3:1], [0:1:1], [0:64:1], [0:31:2], [0:31:2]} | slice | bytes 65536 | tf_op jit(solution)/shard_map/slice | solution.py:55
  153.5 4.9 %slice.265 = bf16[1,1,64,16,16]{2,3,4,1,0:T(8,128)(2,1)} slice(bf16[3,1,64,34,34]{2,3,4,1,0:T(8,128)(2,1)S(1)} %pad.9), slice={[2:3:1], [0:1:1], [0:64:1], [0:31:2], [1:32:2]} | slice | bytes 65536 | tf_op jit(solution)/shard_map/slice | solution.py:55
  158.4 4.9 %slice.266 = bf16[1,1,64,16,16]{2,3,4,1,0:T(8,128)(2,1)} slice(bf16[3,1,64,34,34]{2,3,4,1,0:T(8,128)(2,1)S(1)} %pad.9), slice={[2:3:1], [0:1:1], [0:64:1], [0:31:2], [2:33:2]} | slice | bytes 65536 | tf_op jit(solution)/shard_map/slice | solution.py:55
  163.3 4.9 %slice.267 = bf16[1,1,64,16,16]{2,3,4,1,0:T(8,128)(2,1)} slice(bf16[3,1,64,34,34]{2,3,4,1,0:T(8,128)(2,1)S(1)} %pad.9), slice={[2:3:1], [0:1:1], [0:64:1], [1:32:2], [0:31:2]} | slice | bytes 65536 | tf_op jit(solution)/shard_map/slice | solution.py:55
  168.1 4.9 %slice.268 = bf16[1,1,64,16,16]{2,3,4,1,0:T(8,128)(2,1)} slice(bf16[3,1,64,34,34]{2,3,4,1,0:T(8,128)(2,1)S(1)} %pad.9), slice={[2:3:1], [0:1:1], [0:64:1], [1:32:2], [1:32:2]} | slice | bytes 65536 | tf_op jit(solution)/shard_map/slice | solution.py:55
  173.0 4.9 %slice.269 = bf16[1,1,64,16,16]{2,3,4,1,0:T(8,128)(2,1)} slice(bf16[3,1,64,34,34]{2,3,4,1,0:T(8,128)(2,1)S(1)} %pad.9), slice={[2:3:1], [0:1:1], [0:64:1], [1:32:2], [2:33:2]} | slice | bytes 65536 | tf_op jit(solution)/shard_map/slice | solution.py:55
  177.9 4.9 %slice.270 = bf16[1,1,64,16,16]{2,3,4,1,0:T(8,128)(2,1)} slice(bf16[3,1,64,34,34]{2,3,4,1,0:T(8,128)(2,1)S(1)} %pad.9), slice={[2:3:1], [0:1:1], [0:64:1], [2:33:2], [0:31:2]} | slice | bytes 65536 | tf_op jit(solution)/shard_map/slice | solution.py:55
  183.9 0.8 copy.128
  186.2 1.3 maximum_bitcast_fusion
  193.9 1.0 broadcast_multiply_fusion
  194.9 4.7 %fusion.31 = bf16[2,32,8,5,32]{4,2,3,1,0:T(8,128)(2,1)S(1)} fusion(bf16[3,3,3,32,64]{4,3,2,1,0:T(8,128)(2,1)S(1)} %bitcast.719, bf16[4,64,32,1,7,2]{1,4,5,2,0,3:T(8,128)(2,1)S(1)} %slice.297, bf16[4,64,32,1,8,5]{1,4,5,2,0,3:T(8,128)(2,1)S(1)} %copy.139, pred[8,5]{0,1:T(8,128)(4,1)S(1)} %copy-done.38), kind=kOutput, calls=%fused_computation.28 | convolution fusion | flops 280133632 | bytes 1159208 | tf_op jit(solution)/shard_map/conv_general_dilated | solution.py:29
  199.8 1.1 copy.141
  200.9 1.2 reshape.283
  202.1 258.4 %all-reduce.5.cloned.1.call-done = (f32[27,32,64]{2,1,0:T(8,128)}, f32[27,64,128]{2,1,0:T(8,128)}) async-done(((f32[27,32,64]{2,1,0:T(8,128)}, f32[27,64,128]{2,1,0:T(8,128)}), (f32[27,32,64]{2,1,0:T(8,128)}, f32[27,64,128]{2,1,0:T(8,128)})) %all-reduce.5.cloned.1.call-update) | async-done | bytes 1105936 | tf_op jit(solution)/shard_map/psum | solution.py:111
  460.5 1.9 copy.393
  462.4 0.9 copy.394
  (185 shorter events, 28.5 us)
Async XLA Ops:
  7.2 29.1 %copy-start = (bf16[27,64,128]{2,1,0:T(8,128)(2,1)S(1)}, bf16[27,64,128]{2,1,0:T(8,128)(2,1)}, u32[]{:S(2)}) copy-start(bf16[27,64,128]{2,1,0:T(8,128)(2,1)} %param.7) | copy-start | bytes 1327108
  7.2 12.6 %copy-start.4 = (bf16[2,1,32,1024]{3,2,1,0:T(8,128)(2,1)S(1)}, bf16[2,1,32,1024]{3,2,1,0:T(8,128)(2,1)}, u32[]{:S(2)}) copy-start(bf16[2,1,32,1024]{3,2,1,0:T(8,128)(2,1)} %param.4) | copy-start | bytes 393220
  7.2 10.5 %copy-start.10 = (bf16[1,1,128,256]{3,2,1,0:T(8,128)(2,1)S(1)}, bf16[1,1,128,256]{3,2,1,0:T(8,128)(2,1)}, u32[]{:S(2)}) copy-start(bf16[1,1,128,256]{3,2,1,0:T(8,128)(2,1)} %param.5) | copy-start | bytes 196612
  7.2 453.3 %all-reduce.5.cloned.1.call-start = ((), (), s32[]{:S(2)}) async-start(), calls=%async_computation | async-start | bytes 2654208 | tf_op jit(solution)/shard_map/psum | solution.py:111
  8.8 14.1 %collective-permute-start.1 = (bf16[1,1,32,32,32]{3,2,0,4,1:T(8,128)(2,1)S(1)}, bf16[1,1,32,32,32]{3,2,0,4,1:T(8,128)(2,1)S(1)}, u32[]{:S(2)}, u32[]{:S(2)}) collective-permute-start(bf16[1,1,32,32,32]{3,2,0,4,1:T(8,128)(2,1)S(1)} %copy.119), channel_id=1, source_target_pairs={{1,0},{2,1},{3,2},{4,3},{5,4},{6,5},{7,6},{8,7},{9,8},{10,9},{11,1... | collective-permute-start | bytes 196616 | tf_op jit(solution)/shard_map/ppermute | solution.py:17
  14.6 8.3 %collective-permute-start = (bf16[1,1,32,32,32]{3,2,0,4,1:T(8,128)(2,1)S(1)}, bf16[1,1,32,32,32]{3,2,0,4,1:T(8,128)(2,1)S(1)}, u32[]{:S(2)}, u32[]{:S(2)}) collective-permute-start(bf16[1,1,32,32,32]{3,2,0,4,1:T(8,128)(2,1)S(1)} %copy.118), channel_id=1, source_target_pairs={{0,1},{1,2},{2,3},{3,4},{4,5},{5,6},{6,7},{7,8},{8,9},{9,10},{10,1... | collective-permute-start | bytes 196616 | tf_op jit(solution)/shard_map/ppermute | solution.py:14
  17.8 18.3 %collective-permute-start.3 = (bf16[1,1,128,16,16]{2,4,3,1,0:T(8,128)(2,1)S(1)}, bf16[1,1,128,16,16]{2,4,3,1,0:T(8,128)(2,1)S(1)}, u32[]{:S(2)}, u32[]{:S(2)}) collective-permute-start(bf16[1,1,128,16,16]{2,4,3,1,0:T(8,128)(2,1)S(1)} %bitcast.688), channel_id=1, source_target_pairs={{1,0},{2,1},{3,2},{4,3},{5,4},{6,5},{7,6},{8,7},{9,8},{10,9},{11,1... | collective-permute-start | bytes 196616 | tf_op jit(solution)/shard_map/ppermute | solution.py:25
  21.3 1.9 copy-start.2
  22.9 0.7 copy-start.6
  23.0 0.8 copy-start.8
  24.1 2.9 copy-start.36
  24.1 2.9 copy-start.38
  31.0 29.0 %collective-permute-start.2 = (bf16[1,1,64,32,32]{2,3,4,1,0:T(8,128)(2,1)S(1)}, bf16[1,1,64,32,32]{2,3,4,1,0:T(8,128)(2,1)S(1)}, u32[]{:S(2)}, u32[]{:S(2)}) collective-permute-start(bf16[1,1,64,32,32]{2,3,4,1,0:T(8,128)(2,1)S(1)} %slice_bitcast_fusion.2), channel_id=1, source_target_pairs={{0,1},{1,2},{2,3},{3,4},{4,5},{5,6},{6,7},{7,8},{8,9},{9,10},{10,1... | collective-permute-start | bytes 393224 | tf_op jit(solution)/shard_map/ppermute | solution.py:25
  36.1 0.7 copy-start.39
  38.5 147.7 %collective-permute-start.5 = (bf16[1,1,64,32,32]{2,3,4,0,1:T(8,128)(2,1)S(1)}, bf16[1,1,64,32,32]{2,3,4,0,1:T(8,128)(2,1)}, u32[]{:S(2)}, u32[]{:S(2)}) collective-permute-start(bf16[1,1,64,32,32]{2,3,4,0,1:T(8,128)(2,1)S(1)} %get-tuple-element.22), channel_id=1, source_target_pairs={{1,0},{2,1},{3,2},{4,3},{5,4},{6,5},{7,6},{8,7},{9,8},{10,9},{11,1... | collective-permute-start | bytes 393224 | tf_op jit(solution)/shard_map/ppermute | solution.py:17
  40.5 145.8 %collective-permute-start.4 = (bf16[1,1,64,32,32]{2,3,4,0,1:T(8,128)(2,1)S(1)}, bf16[1,1,64,32,32]{2,3,4,0,1:T(8,128)(2,1)}, u32[]{:S(2)}, u32[]{:S(2)}) collective-permute-start(bf16[1,1,64,32,32]{2,3,4,0,1:T(8,128)(2,1)S(1)} %get-tuple-element.21), channel_id=1, source_target_pairs={{0,1},{1,2},{2,3},{3,4},{4,5},{5,6},{6,7},{7,8},{8,9},{9,10},{10,1... | collective-permute-start | bytes 393224 | tf_op jit(solution)/shard_map/ppermute | solution.py:14
  46.3 1.0 copy-start.3
  46.3 1.1 copy-start.9
  51.1 1.0 copy-start.1
  55.7 1.0 copy-start.7
  183.9 0.9 copy-start.40
  187.8 0.8 copy-start.35
  187.8 1.0 copy-start.34
  188.3 0.9 copy-start.33
  188.3 1.0 copy-start.32
  188.3 1.2 copy-start.31
  188.3 1.4 copy-start.30
  188.3 1.6 copy-start.29
  188.4 1.8 copy-start.28
  188.4 1.9 copy-start.27
  188.5 2.0 copy-start.26
  188.5 2.2 copy-start.25
  188.5 2.4 copy-start.24
  188.8 2.3 copy-start.23
  189.2 2.1 copy-start.22
  189.4 2.1 copy-start.21
  189.5 2.1 copy-start.20
  189.7 2.1 copy-start.19
  189.9 2.1 copy-start.18
  190.1 2.1 copy-start.17
  190.3 2.1 copy-start.16
  190.5 2.1 copy-start.15
  190.7 2.1 copy-start.14
  190.9 2.1 copy-start.13
  191.1 2.0 copy-start.12
  191.3 2.0 copy-start.11
  193.9 1.0 copy-start.37
  460.5 1.9 copy-start.5
Sparse Core Ops, SparseCore 0:
  195.0 265.4 all-reduce.4
where the time goes:
time: 471 us; the launch traced here: 470 us
  waiting for transfers between devices  258 us (55%)
  local copies, waits for them, and re-layouts  143 us (30%)
  matrix products  28.3 us (6%)
  starting transfers between devices  21.4 us (5%)
  between operations  15.2 us (3%)
    psum x1, waiting for transfers between devices, local(): first_grads = lax.psum(first_grads, ('sample', 'space'))  258 us
    slice x27, local copies, waits for them, and re-layouts, weight_grad(): lax.slice(padded, (depth_tap, 0, 0, row_tap, col_tap), (depth_tap + strid...  123 us
    dot_general x54, matrix products, weight_grad(): jnp.einsum('zbiyx,zboyx->io', window, grads, preferred_element_type=jnp.f...  18.3 us
    conv_general_dilated x4, matrix products, convolve(): lax.conv_general_dilated(inputs, kernel, (stride, stride, stride), margin...  9.99 us
  transfers between devices with their start and end apart: 7, of which 1 were waited for; matrix products, arithmetic and copies ran while one was open for 34% of the time, Pallas kernels for 0%

commit v1 on v0

--- a/solution.py
+++ b/solution.py
@@ -4,6 +4,11 @@
 from jax.sharding import PartitionSpec as P
 
 SIDE = 32
+
+
+def summed_here(x, mesh_axis):
+    parts = lax.all_gather(x, mesh_axis)
+    return jnp.sum(parts, axis=0)
 
 
 def with_halo(block, sides, width):
@@ -108,7 +113,7 @@
     ).astype(jnp.bfloat16)
     padded_input = jnp.pad(framed, ((0, 0), (0, 0), (0, 0), (1, 1), (1, 1)))
     first_grads = weight_grad(padded_input, pre_grads, 1) * scale_one
-    first_grads = lax.psum(first_grads, ("sample", "space"))
+    first_grads = summed_here(first_grads, ("sample", "space"))
     return (
         layer_out,
         input_grads.reshape(depth, batch, channels_in, plane),

time: 471 us -> 947 us (2.01)
  waiting for transfers between devices: 258 us -> 699 us
  other arithmetic: 3.85 us -> 39.3 us
    all_gather x0 -> x1, waiting for transfers between devices: none -> 475 us  [summed_here(): parts = lax.all_gather(x, mesh_axis)]
    reduce_sum x0 -> x1, other arithmetic: none -> 35.4 us  [summed_here(): return jnp.sum(parts, axis=0)]
    psum x1, waiting for transfers between devices: 258 us -> 224 us  [local(): second_grads = lax.psum(local_two, ('sample', 'space'))]
  transfers between devices with their start and end apart: 7 -> 8, of which waited for: 1 -> 2; matrix products, arithmetic and copies ran while one was open for 34% -> 20% of each run, Pallas kernels for 0% -> 0%
where the time goes in v1:
time: 947 us; the launch traced here: 946 us
  waiting for transfers between devices  699 us (74%)
  local copies, waits for them, and re-layouts  143 us (15%)
  other arithmetic  39.3 us (4%)
  matrix products  28.5 us (3%)
  starting transfers between devices  21.2 us (2%)
  between operations  15.3 us (2%)
    all_gather x1, waiting for transfers between devices, summed_here(): parts = lax.all_gather(x, mesh_axis)  475 us
    psum x1, waiting for transfers between devices, local(): second_grads = lax.psum(local_two, ('sample', 'space'))  224 us
    slice x27, local copies, waits for them, and re-layouts, weight_grad(): lax.slice(padded, (depth_tap, 0, 0, row_tap, col_tap), (depth_tap + strid...  123 us
    reduce_sum x1, other arithmetic, summed_here(): return jnp.sum(parts, axis=0)  35.4 us
  transfers between devices with their start and end apart: 8, of which 2 were waited for; matrix products, arithmetic and copies ran while one was open for 20% of the time, Pallas kernels for 0%

profile of v1, /device:TPU:1, one launch (start us, length us, event | category | flops | bytes accessed | tf_op | source)
XLA Modules:
  0.0 946.0 jit_solution(15627307449861322594)
XLA Ops:
  7.2 0.9 fusion.282
  8.8 5.1 collective-permute-start.1
  14.6 3.1 collective-permute-start
  17.8 1.9 collective-permute-start.3
  20.5 0.9 copy.204
  21.4 1.6 copy.241
  24.1 1.6 copy.207
  25.7 1.2 slice.285
  26.9 3.8 add_divide_fusion
  31.9 0.8 fusion.24
  47.9 0.8 broadcast_multiply_fusion.1
  49.0 4.5 collective-permute-start.2
  54.3 1.9 collective-permute-start.5
  56.2 4.5 collective-permute-start.4
  61.3 4.9 slice.246
  66.3 4.9 slice.247
  71.1 4.9 slice.248
  76.0 4.9 slice.249
  80.9 4.9 slice.250
  85.8 4.9 slice.251
  90.6 4.9 slice.252
  95.5 4.9 slice.253
  100.4 4.9 slice.254
  105.3 4.9 slice.255
  110.2 4.9 slice.256
  115.0 4.9 slice.257
  119.9 4.9 slice.258
  124.8 4.9 slice.259
  129.7 4.9 slice.260
  134.6 4.9 slice.261
  139.4 4.9 slice.262
  144.3 4.9 slice.263
  149.2 4.9 slice.264
  154.1 4.9 slice.265
  158.9 4.9 slice.266
  163.8 4.9 slice.267
  168.7 4.9 slice.268
  173.6 4.9 slice.269
  178.4 4.9 slice.270
  186.0 1.3 maximum_bitcast_fusion
  193.7 1.0 broadcast_multiply_fusion
  194.7 4.7 fusion.31
  200.4 1.1 copy.225
  201.5 1.2 reshape.664
  202.7 474.6 %all-gather.2.cloned.1.call-done = f32[256,27,32,64]{3,2,1,0:T(8,128)} async-done(((f32[1,27,32,64]{3,2,1,0:T(8,128)}), f32[256,27,32,64]{3,2,1,0:T(8,128)}) %all-gather.2.cloned.1.call-update) | async-done | bytes 56623120 | tf_op jit(solution)/shard_map/all_gather | solution.py:10
  677.3 35.4 %reduce_sum.9 = f32[27,32,64]{2,1,0:T(8,128)} reduce(f32[256,27,32,64]{3,2,1,0:T(8,128)} %all-gather.2.cloned.1.call-done, f32[]{:T(128)} %constant.4.clone.1), dimensions={0}, to_apply=%region_0.1 | reduce | flops 14100480 | bytes 56844292 | tf_op jit(solution)/shard_map/reduce_sum | solution.py:11
  712.7 224.3 %all-reduce.4.cloned.1.call-done = f32[27,64,128]{2,1,0:T(8,128)} async-done(((f32[27,64,128]{2,1,0:T(8,128)}), f32[27,64,128]{2,1,0:T(8,128)}) %all-reduce.4.cloned.1.call-update) | async-done | bytes 884752 | tf_op jit(solution)/shard_map/psum | solution.py:104
  937.0 2.2 copy.476
  (186 shorter events, 30.2 us)
Async XLA Ops:
  7.2 24.3 %copy-start = (bf16[27,64,128]{2,1,0:T(8,128)(2,1)S(1)}, bf16[27,64,128]{2,1,0:T(8,128)(2,1)}, u32[]{:S(2)}) copy-start(bf16[27,64,128]{2,1,0:T(8,128)(2,1)} %param.7) | copy-start | bytes 1327108
  7.2 12.6 %copy-start.4 = (bf16[2,1,32,1024]{3,2,1,0:T(8,128)(2,1)S(1)}, bf16[2,1,32,1024]{3,2,1,0:T(8,128)(2,1)}, u32[]{:S(2)}) copy-start(bf16[2,1,32,1024]{3,2,1,0:T(8,128)(2,1)} %param.4) | copy-start | bytes 393220
  7.2 10.5 %copy-start.9 = (bf16[1,1,128,256]{3,2,1,0:T(8,128)(2,1)S(1)}, bf16[1,1,128,256]{3,2,1,0:T(8,128)(2,1)}, u32[]{:S(2)}) copy-start(bf16[1,1,128,256]{3,2,1,0:T(8,128)(2,1)} %param.5) | copy-start | bytes 196612
  7.2 670.1 %all-gather.2.cloned.1.call-start = ((), (), s32[]{:S(2)}) async-start(), calls=%async_computation | async-start | bytes 113688576 | tf_op jit(solution)/shard_map/all_gather | solution.py:10
  8.8 14.1 %collective-permute-start.1 = (bf16[1,1,32,32,32]{3,2,0,4,1:T(8,128)(2,1)S(1)}, bf16[1,1,32,32,32]{3,2,0,4,1:T(8,128)(2,1)S(1)}, u32[]{:S(2)}, u32[]{:S(2)}) collective-permute-start(bf16[1,1,32,32,32]{3,2,0,4,1:T(8,128)(2,1)S(1)} %copy.203), channel_id=1, source_target_pairs={{1,0},{2,1},{3,2},{4,3},{5,4},{6,5},{7,6},{8,7},{9,8},{10,9},{11,1... | collective-permute-start | bytes 196616 | tf_op jit(solution)/shard_map/ppermute | solution.py:22
  14.6 8.3 collective-permute-start
  17.8 13.5 %collective-permute-start.3 = (bf16[1,1,128,16,16]{2,4,3,1,0:T(8,128)(2,1)S(1)}, bf16[1,1,128,16,16]{2,4,3,1,0:T(8,128)(2,1)S(1)}, u32[]{:S(2)}, u32[]{:S(2)}) collective-permute-start(bf16[1,1,128,16,16]{2,4,3,1,0:T(8,128)(2,1)S(1)} %bitcast.688), channel_id=1, source_target_pairs={{1,0},{2,1},{3,2},{4,3},{5,4},{6,5},{7,6},{8,7},{9,8},{10,9},{11,1... | collective-permute-start | bytes 196616 | tf_op jit(solution)/shard_map/ppermute | solution.py:30
  21.3 1.9 copy-start.2
  22.9 0.7 copy-start.5
  22.9 0.8 copy-start.7
  24.1 2.8 copy-start.35
  24.1 2.8 copy-start.37
  31.3 0.7 copy-start.38
  34.7 1.0 copy-start.3
  34.8 1.1 copy-start.8
  39.5 1.0 copy-start.1
  44.4 1.0 copy-start.6
  48.7 888.2 %all-reduce.4.cloned.1.call-start = ((), (), s32[]{:S(2)}) async-start(), calls=%async_computation.1 | async-start | bytes 1769472 | tf_op jit(solution)/shard_map/psum | solution.py:104
  49.0 11.8 %collective-permute-start.2 = (bf16[1,1,64,32,32]{2,3,4,1,0:T(8,128)(2,1)S(1)}, bf16[1,1,64,32,32]{2,3,4,1,0:T(8,128)(2,1)S(1)}, u32[]{:S(2)}, u32[]{:S(2)}) collective-permute-start(bf16[1,1,64,32,32]{2,3,4,1,0:T(8,128)(2,1)S(1)} %slice_bitcast_fusion.2), channel_id=1, source_target_pairs={{0,1},{1,2},{2,3},{3,4},{4,5},{5,6},{6,7},{7,8},{8,9},{9,10},{10,1... | collective-permute-start | bytes 393224 | tf_op jit(solution)/shard_map/ppermute | solution.py:30
  54.3 131.6 %collective-permute-start.5 = (bf16[1,1,64,32,32]{2,3,4,0,1:T(8,128)(2,1)}, bf16[1,1,64,32,32]{2,3,4,0,1:T(8,128)(2,1)}, u32[]{:S(2)}, u32[]{:S(2)}) collective-permute-start(bf16[1,1,64,32,32]{2,3,4,0,1:T(8,128)(2,1)} %get-tuple-element.24), channel_id=1, source_target_pairs={{1,0},{2,1},{3,2},{4,3},{5,4},{6,5},{7,6},{8,7},{9,8},{10,9},{11,1... | collective-permute-start | bytes 393224 | tf_op jit(solution)/shard_map/ppermute | solution.py:22
  56.2 129.7 %collective-permute-start.4 = (bf16[1,1,64,32,32]{2,3,4,0,1:T(8,128)(2,1)S(1)}, bf16[1,1,64,32,32]{2,3,4,0,1:T(8,128)(2,1)}, u32[]{:S(2)}, u32[]{:S(2)}) collective-permute-start(bf16[1,1,64,32,32]{2,3,4,0,1:T(8,128)(2,1)S(1)} %get-tuple-element.23), channel_id=1, source_target_pairs={{0,1},{1,2},{2,3},{3,4},{4,5},{5,6},{6,7},{7,8},{8,9},{9,10},{10,1... | collective-permute-start | bytes 393224 | tf_op jit(solution)/shard_map/ppermute | solution.py:19
  184.4 0.9 copy-start.39
  187.6 0.8 copy-start.34
  187.6 1.0 copy-start.33
  188.1 0.9 copy-start.32
  188.1 1.0 copy-start.31
  188.1 1.2 copy-start.30
  188.1 1.4 copy-start.29
  188.1 1.6 copy-start.28
  188.2 1.8 copy-start.27
  188.2 1.9 copy-start.26
  188.3 2.0 copy-start.25
  188.3 2.2 copy-start.24
  188.3 2.4 copy-start.23
  188.6 2.3 copy-start.22
  189.0 2.1 copy-start.21
  189.1 2.1 copy-start.20
  189.3 2.1 copy-start.19
  189.5 2.1 copy-start.18
  189.7 2.1 copy-start.17
  189.9 2.1 copy-start.16
  190.1 2.1 copy-start.15
  190.3 2.1 copy-start.14
  190.5 2.1 copy-start.13
  190.7 2.1 copy-start.12
  190.9 2.0 copy-start.11
  191.1 2.0 copy-start.10
  193.2 1.6 copy-start.36
Sparse Core Ops, SparseCore 0:
  48.9 628.3 all-gather.1
  683.3 253.6 all-reduce.3
